TPU v7x, 512 devices: a whole 4x8x8 slice. The times are simulated.
512 devices in a mesh: seq: 128 (over z, y, core), tp: 4 (over x).
Axes of the slice: x: 4, y: 8, z: 8, core: 2. Of those that a mesh axis runs over, the one named last changes fastest.
Arguments:
- hidden_in: bfloat16 [16384, 1536], P('seq'), may hold values from -6 to 6
- w_query: bfloat16 [1536, 1536], P(None, 'tp'), may hold values from -0.625 to 0.625
- key_weight: bfloat16 [1536, 512], P(None, 'tp'), may hold values from -0.625 to 0.625
- value_weight: bfloat16 [1536, 512], P(None, 'tp'), may hold values from -0.15625 to 0.15625
- w_out: bfloat16 [1536, 1536], P('tp'), may hold values from -0.4375 to 0.4375
- cached_prefix_keys: bfloat16 [4096, 512], P('seq', 'tp'), may hold values from -60000 to 60000
- cached_prefix_values: bfloat16 [4096, 512], P('seq', 'tp'), may hold values from -6 to 6
- doc_ids: int32 [128, 128], P('seq'), may hold values from 0 to 3, never falling along the last dimension, each value on 1 to 64 neighbouring positions
- routes: int32 [16384, 8], P(('seq', 'tp')), may hold values from 0 to 31, all different within a row; in each aligned block of 32 rows (0 to 31, 32 to 63, ...) at most 16 rows name the same one
- gate_scores: float32 [16384, 8], P(('seq', 'tp')), may hold values from 0.2 to 1
- expert_in: bfloat16 [128, 1536, 256], P('seq'), may hold values from -0.15625 to 0.15625
- expert_out: bfloat16 [128, 128, 1536], P('seq'), may hold values from -0.25 to 0.25
Outputs:
- attn_proj: bfloat16 [16384, 1536], P(('seq', 'tp'))
- expert_mix: bfloat16 [16384, 1536], P(('seq', 'tp'))
- layer_out: bfloat16 [16384, 1536], P(('seq', 'tp'))
Inputs may be any that keep to these rules, and one draw needn't show every extreme that they name: `routes`: within the rows of one device (aligned blocks of 32 tokens) no expert is picked by more than 16 tokens, a bound that some block reaches; every expert is picked somewhere.
All inputs are finite; a program needn't handle non-finite values.
Results may differ from a plain program's by a relative error of at most 0.028.
Values may be sent and summed in bfloat16 or wider, within the bound.
No kernel may reach another device: no remote copies, remote signals or barrier semaphores. Data moves between devices by JAX's collectives and lax.ppermute only.
A program may use at most 64 MiB of HBM per device.

v0:
```python
import jax
import jax.numpy as jnp
from jax import lax
from jax.sharding import PartitionSpec as P

HEAD_WIDTH = 64
EXPERTS = 32
EPSILON = 1e-06
RESIDUAL = 0.22


def normalize(values):
    values = values.astype(jnp.float32)
    return values * lax.rsqrt(jnp.mean(values * values, axis=-1, keepdims=True) + EPSILON)


def rotary_apply(values, token_positions):
    half_size = values.shape[-1] // 2
    frequency = jnp.exp(
        -jnp.log(10000.0) * jnp.arange(half_size, dtype=jnp.float32) * 2.0 / values.shape[-1]
    )
    angles = token_positions[:, None] * frequency[None, :]
    cosine = jnp.cos(angles)[:, None, :]
    sine_part = jnp.sin(angles)[:, None, :]
    first_half = values[..., :half_size]
    second = values[..., half_size:]
    return jnp.concatenate(
        [first_half * cosine - second * sine_part, second * cosine + first_half * sine_part],
        axis=-1,
    )


def body(
    hidden_in,
    w_query,
    key_weight,
    value_weight,
    w_out,
    cached_prefix_keys,
    cached_prefix_values,
    doc_ids,
    routes,
    gate_scores,
    expert_in,
    expert_out,
):
    rows_dev = hidden_in.shape[0]
    column_list = hidden_in.shape[1]
    head_size = HEAD_WIDTH
    kv_local = key_weight.shape[1] // head_size
    group_width = w_query.shape[1] // head_size // kv_local
    seq_count = lax.axis_size("seq")
    prefix_len = cached_prefix_keys.shape[0] * seq_count
    doc_row = doc_ids[0]
    row_index = jnp.arange(rows_dev, dtype=jnp.int32)
    same_doc = doc_row[:, None] == doc_row[None, :]
    doc_start = jnp.min(jnp.where(same_doc, row_index[None, :], rows_dev), axis=1)
    token_positions = (prefix_len + row_index - doc_start).astype(jnp.float32)
    normed_input = normalize(hidden_in).astype(jnp.bfloat16)
    query_rows_all = jnp.dot(normed_input, w_query, preferred_element_type=jnp.float32).reshape(
        rows_dev, kv_local * group_width, head_size
    )
    query_rows_all = (
        rotary_apply(query_rows_all, token_positions)
        .astype(jnp.bfloat16)
        .reshape(rows_dev, kv_local, group_width, head_size)
    )
    fresh_key = jnp.dot(normed_input, key_weight, preferred_element_type=jnp.float32).reshape(
        rows_dev, kv_local, head_size
    )
    fresh_key = rotary_apply(fresh_key, token_positions).astype(jnp.bfloat16)
    fresh_value = (
        jnp.dot(normed_input, value_weight, preferred_element_type=jnp.float32)
        .astype(jnp.bfloat16)
        .reshape(rows_dev, kv_local, head_size)
    )
    own_scores = (
        jnp.einsum("tkgd,skd->tkgs", query_rows_all, fresh_key, preferred_element_type=jnp.float32)
        / head_size
    )
    visible = same_doc & (row_index[None, :] <= row_index[:, None])
    own_scores = jnp.where(visible[:, None, None, :], own_scores, -jnp.inf)
    row_top = jnp.max(own_scores, axis=-1)
    weights = jnp.exp(own_scores - row_top[..., None])
    denominator = jnp.sum(weights, axis=-1)
    numerator = jnp.einsum(
        "tkgs,skd->tkgd",
        weights.astype(jnp.bfloat16),
        fresh_value,
        preferred_element_type=jnp.float32,
    )
    running = (row_top, denominator, numerator)
    whole_keys, whole_values = (
        lax.all_gather(cached_prefix_keys, "seq", axis=0, tiled=True),
        lax.all_gather(cached_prefix_values, "seq", axis=0, tiled=True),
    )
    top_old, denom_old, numer_old = running
    key_rows = whole_keys.reshape(-1, kv_local, head_size)
    value_rows = whole_values.reshape(-1, kv_local, head_size)
    scores = (
        jnp.einsum("tkgd,pkd->tkgp", query_rows_all, key_rows, preferred_element_type=jnp.float32)
        / head_size
    )
    top_new = jnp.maximum(top_old, jnp.max(scores, axis=-1))
    shrink = jnp.exp(top_old - top_new)
    part_weights = jnp.exp(scores - top_new[..., None])
    denom_new = denom_old * shrink + jnp.sum(part_weights, axis=-1)
    numer_new = numer_old * shrink[..., None] + jnp.einsum(
        "tkgp,pkd->tkgd",
        part_weights.astype(jnp.bfloat16),
        value_rows,
        preferred_element_type=jnp.float32,
    )
    running = (top_new, denom_new, numer_new)
    attended = (
        (running[2] / running[1][..., None])
        .astype(jnp.bfloat16)
        .reshape(rows_dev, kv_local * group_width * head_size)
    )
    moe_rows = routes.shape[0]
    row_start = lax.axis_index("tp") * moe_rows
    summed_all = lax.psum(jnp.dot(attended, w_out, preferred_element_type=jnp.float32), "tp")
    attn_sum = lax.dynamic_slice_in_dim(summed_all, row_start, moe_rows, 0)
    residual = (
        lax.dynamic_slice_in_dim(hidden_in, row_start, moe_rows, 0).astype(jnp.float32)
        + RESIDUAL * attn_sum
    )
    routed = normalize(residual).astype(jnp.bfloat16)
    experts = EXPERTS
    units_dev = expert_in.shape[0]
    hparts = units_dev * seq_count // experts
    capacity = moe_rows // 2
    ff_part = expert_out.shape[1]
    onehot = (routes[:, :, None] == jnp.arange(experts, dtype=jnp.int32)[None, None, :]).astype(
        jnp.int32
    )
    per_row = jnp.sum(onehot, axis=1)
    before = jnp.cumsum(per_row, axis=0) - per_row
    rank_in = jnp.sum(onehot * before[:, None, :], axis=2)
    slot_of = routes * capacity + rank_in
    slot_ids = jnp.arange(experts * capacity, dtype=jnp.int32)
    pick_hit = slot_of[:, :, None] == slot_ids[None, None, :]
    selector = jnp.any(pick_hit, axis=1).T.astype(jnp.bfloat16)
    combiner = jnp.sum(jnp.where(pick_hit, gate_scores[:, :, None], 0.0), axis=1)
    gathered = jnp.dot(selector, routed, preferred_element_type=jnp.float32).astype(jnp.bfloat16)
    outgoing = jnp.broadcast_to(
        gathered.reshape(experts, 1, capacity, column_list),
        (experts, hparts, capacity, column_list),
    )
    outgoing = outgoing.reshape(seq_count, units_dev, capacity, column_list)
    gate_up = jnp.einsum(
        "sucd,udf->sucf",
        lax.all_to_all(outgoing, "seq", split_axis=0, concat_axis=0, tiled=True),
        expert_in,
        preferred_element_type=jnp.float32,
    )
    activated = (jax.nn.silu(gate_up[..., :ff_part]) * gate_up[..., ff_part:]).astype(jnp.bfloat16)
    partial_value = jnp.einsum(
        "sucf,ufd->sucd", activated, expert_out, preferred_element_type=jnp.float32
    ).astype(jnp.bfloat16)
    returned = lax.all_to_all(partial_value, "seq", split_axis=0, concat_axis=0, tiled=True)
    part_sum = jnp.sum(
        returned.reshape(experts, hparts, capacity, column_list).astype(jnp.float32), axis=1
    )
    part_sum = part_sum.reshape(experts * capacity, column_list)
    expert_sum = jnp.dot(
        combiner, part_sum, precision=lax.Precision.HIGHEST, preferred_element_type=jnp.float32
    )
    layer_out = (residual + RESIDUAL * expert_sum).astype(jnp.bfloat16)
    return (attn_sum.astype(jnp.bfloat16), expert_sum.astype(jnp.bfloat16), layer_out)


def solution(mesh):
    in_specs = (
        P("seq", None),
        P(None, "tp"),
        P(None, "tp"),
        P(None, "tp"),
        P("tp", None),
        P("seq", "tp"),
        P("seq", "tp"),
        P("seq", None),
        P(("seq", "tp"), None),
        P(("seq", "tp"), None),
        P("seq", None, None),
        P("seq", None, None),
    )
    out_specs = (P(("seq", "tp"), None), P(("seq", "tp"), None), P(("seq", "tp"), None))
    return jax.shard_map(body, mesh=mesh, in_specs=in_specs, out_specs=out_specs, check_vma=False)
```

profile of v0, /device:TPU:17, one launch (start us, length us, event | category | flops | bytes accessed | tf_op | source)
XLA Modules:
  0.0 620.2 jit_solution(3944682123108635875)
XLA Ops:
  7.2 0.0 copy-start
  7.2 0.0 all-gather.3.cloned.1.call-start
  7.2 0.7 all-gather.3.cloned.1.call-update
  7.9 0.0 all-gather.5.cloned.1.call-start
  8.0 0.7 all-gather.5.cloned.1.call-update
  8.7 0.0 all-reduce.2.cloned.1.call-start
  8.7 1.2 fusion.21
  9.9 0.8 fusion.33
  10.7 2.0 fusion.43
  12.7 1.5 fusion.45
  14.2 0.1 multiply_cosine_fusion
  14.4 0.8 compare_and_fusion
  15.2 0.3 fusion.48
  15.5 0.1 fusion.28
  15.6 1.5 convolution_convert_fusion.1
  17.1 77.1 %all-gather.3.cloned.1.call-done = bf16[4096,128]{1,0:T(8,128)(2,1)} async-done(((bf16[32,128]{1,0:T(8,128)(2,1)}), bf16[4096,128]{1,0:T(8,128)(2,1)}) %all-gather.3.cloned.1.call-update) | async-done | bytes 1048592 | tf_op jit(solution)/shard_map/all_gather | solution.py:94
  94.2 1.5 copy.68
  95.7 1.9 bitcast_reduce_fusion
  97.6 4.6 copy-done.1
  102.2 2.2 fusion.1
  104.3 67.8 %all-gather.5.cloned.1.call-done = bf16[4096,128]{1,0:T(8,128)(2,1)} async-done(((bf16[32,128]{1,0:T(8,128)(2,1)}), bf16[4096,128]{1,0:T(8,128)(2,1)}) %all-gather.5.cloned.1.call-update) | async-done | bytes 1048592 | tf_op jit(solution)/shard_map/all_gather | solution.py:95
  172.1 1.5 copy.69
  173.7 5.9 fusion.16
  179.6 0.2 fusion.19
  179.8 1.3 fusion.49
  181.1 0.0 all-reduce.2.cloned.1.call-update
  181.1 0.1 copy.70
  181.2 0.1 convert_reduce_fusion.1
  181.3 0.1 reduce_window_sum.11
  181.4 0.7 select_reduce_fusion.1
  182.1 0.1 copy.71
  182.2 0.1 copy.72
  182.2 0.2 fusion.26
  182.5 48.2 %all-reduce.2.cloned.1.call-done = f32[128,1536]{1,0:T(8,128)} async-done(((f32[128,1536]{1,0:T(8,128)}), f32[128,1536]{1,0:T(8,128)}) %all-reduce.2.cloned.1.call-update) | async-done | bytes 786448 | tf_op jit(solution)/shard_map/psum | solution.py:122
  230.7 1.1 multiply_reduce_fusion
  231.7 1.6 convolution_convert_fusion
  233.3 0.8 broadcast_in_dim.40
  234.1 158.0 %all_to_all.10 = bf16[128,1,16,1536]{3,2,1,0:T(8,128)(2,1)S(1)} all-to-all(bf16[128,1,16,1536]{3,2,1,0:T(8,128)(2,1)S(1)} %bitcast.102), channel_id=1, replica_groups=mesh['seq'=128,'tp'=4] {'seq'}, dimensions={0} | all-to-all | bytes 12582912 | tf_op jit(solution)/shard_map/all_to_all | solution.py:153
  392.1 7.3 %fusion.8 = f32[128,1,16,256]{3,0,2,1:T(8,128)S(1)} fusion(bf16[128,1,16,1536]{3,2,1,0:T(8,128)(2,1)S(1)} %all_to_all.10, bf16[1,1536,256]{2,1,0:T(8,128)(2,1)S(1)} %copy-done.6), kind=kOutput, calls=%fused_computation.12 | convolution fusion | flops 1610612736 | bytes 9175040 | tf_op jit(solution)/shard_map/sucd,udf->sucf/dot_general | solution.py:151
  399.4 1.8 convert_bitcast_fusion
  401.2 6.4 %copy.75 = bf16[128,1,16,1536]{3,2,1,0:T(8,128)(2,1)} copy(bf16[128,1,16,1536]{3,0,2,1:T(8,128)(2,1)S(1)} %convert_bitcast_fusion) | data formatting | bytes 12582912 | tf_op jit(solution)/shard_map/convert_element_type | solution.py:160
  407.6 21.8 %all-to-all-start.1 = ((bf16[128,1,16,1536]{3,2,1,0:T(8,128)(2,1)}), bf16[128,1,16,1536]{3,2,1,0:T(8,128)(2,1)}, u32[]{:S(2)}, u32[]{:S(2)}) async-start(bf16[128,1,16,1536]{3,2,1,0:T(8,128)(2,1)} %copy.75), calls=%async_computation.1 | async-start | bytes 12582912 | tf_op jit(solution)/shard_map/all_to_all | solution.py:161
  429.4 0.1 copy.73
  429.5 0.2 select_reduce_fusion
  429.7 1.6 dynamic-slice_convert_fusion
  431.3 174.6 %all-to-all-done.1 = bf16[128,1,16,1536]{3,2,1,0:T(8,128)(2,1)} async-done(((bf16[128,1,16,1536]{3,2,1,0:T(8,128)(2,1)}), bf16[128,1,16,1536]{3,2,1,0:T(8,128)(2,1)}, u32[]{:S(2)}, u32[]{:S(2)}) %all-to-all-start.1) | async-done | bytes 6291488 | tf_op jit(solution)/shard_map/all_to_all | solution.py:161
  605.9 4.3 convert_reduce_fusion
  610.2 3.5 add_convert_fusion
  (22 shorter events, 0.1 us)
Async XLA Ops:
  7.2 172.6 %copy-start = (bf16[384,1536]{1,0:T(8,128)(2,1)S(1)}, bf16[384,1536]{1,0:T(8,128)(2,1)}, u32[]{:S(2)}) copy-start(bf16[384,1536]{1,0:T(8,128)(2,1)} %param.16) | copy-start | bytes 3538948
  7.2 87.0 %all-gather.3.cloned.1.call-start = ((), (), s32[]{:S(2)}) async-start(), calls=%async_computation.2 | async-start | bytes 1056768 | tf_op jit(solution)/shard_map/all_gather | solution.py:94
  7.9 164.2 %all-gather.5.cloned.1.call-start = ((), (), s32[]{:S(2)}) async-start(), calls=%async_computation.3 | async-start | bytes 1056768 | tf_op jit(solution)/shard_map/all_gather | solution.py:95
  8.7 222.0 %all-reduce.2.cloned.1.call-start = ((), (), s32[]{:S(2)}) async-start(), calls=%async_computation.4 | async-start | bytes 1572864 | tf_op jit(solution)/shard_map/psum | solution.py:122
  97.6 4.6 copy-start.1
  173.6 7.5 %copy-start.4 = (s32[32,8]{0,1:T(8,128)S(1)}, s32[32,8]{0,1:T(8,128)}, u32[]{:S(2)}) copy-start(s32[32,8]{0,1:T(8,128)} %param.20) | copy-start | bytes 3076
  173.6 57.0 %copy-start.2 = (bf16[128,1536]{1,0:T(8,128)(2,1)S(1)}, bf16[128,1536]{1,0:T(8,128)(2,1)}, u32[]{:S(2)}) copy-start(bf16[128,1536]{1,0:T(8,128)(2,1)} %param.12) | copy-start | bytes 1179652
  234.1 158.0 %copy-start.6 = (bf16[1,1536,256]{2,1,0:T(8,128)(2,1)S(1)}, bf16[1,1536,256]{2,1,0:T(8,128)(2,1)}, u32[]{:S(2)}) copy-start(bf16[1,1536,256]{2,1,0:T(8,128)(2,1)} %param.22) | copy-start | bytes 2359300
  392.1 7.3 %copy-start.3 = (bf16[1,128,1536]{2,1,0:T(8,128)(2,1)S(1)}, bf16[1,128,1536]{2,1,0:T(8,128)(2,1)}, u32[]{:S(2)}) copy-start(bf16[1,128,1536]{2,1,0:T(8,128)(2,1)} %param.23) | copy-start | bytes 1179652
  407.6 21.8 %copy-start.5 = (f32[32,8]{0,1:T(8,128)S(1)}, f32[32,8]{0,1:T(8,128)}, u32[]{:S(2)}) copy-start(f32[32,8]{0,1:T(8,128)} %param.21) | copy-start | bytes 3076
  407.6 198.3 %all-to-all-start.1 = ((bf16[128,1,16,1536]{3,2,1,0:T(8,128)(2,1)}), bf16[128,1,16,1536]{3,2,1,0:T(8,128)(2,1)}, u32[]{:S(2)}, u32[]{:S(2)}) async-start(bf16[128,1,16,1536]{3,2,1,0:T(8,128)(2,1)} %copy.75), calls=%async_computation.1 | async-start | bytes 12582912 | tf_op jit(solution)/shard_map/all_to_all | solution.py:161
Sparse Core Ops, SparseCore 0:
  11.0 83.1 all-gather.2
  97.2 74.8 all-gather.4
  181.2 49.3 all-reduce.1
where the time goes:
time: 621 us; the launch traced here: 620 us
  waiting for transfers between devices  369 us (59%)
  blocking collectives  158 us (25%)
  matrix products  28.7 us (5%)
  starting transfers between devices  21.9 us (4%)
  local copies, waits for them, and re-layouts  16.6 us (3%)
  between operations  14 us (2%)
  other arithmetic  11.9 us (2%)
    all_to_all x1, waiting for transfers between devices, body(): lax.all_to_all(partial_value, 'seq', split_axis=0, concat_axis=0, tiled=T...  175 us
    all_to_all x1, blocking collectives, body(): lax.all_to_all(outgoing, 'seq', split_axis=0, concat_axis=0, tiled=True)  158 us
    all_gather x1, waiting for transfers between devices, body(): lax.all_gather(cached_prefix_keys, 'seq', axis=0, tiled=True)  77.1 us
    all_gather x1, waiting for transfers between devices, body(): lax.all_gather(cached_prefix_values, 'seq', axis=0, tiled=True)  67.8 us
    psum x1, waiting for transfers between devices, body(): lax.psum(jnp.dot(attended, w_out, preferred_element_type=jnp.float32), 'tp')  48.2 us
    all_to_all x1, starting transfers between devices, body(): lax.all_to_all(partial_value, 'seq', split_axis=0, concat_axis=0, tiled=T...  21.8 us
  transfers between devices with their start and end apart: 4, of which 4 were waited for; matrix products, arithmetic and copies ran while one was open for 3% of the time, Pallas kernels for 0%

commit v1 on v0

--- a/solution.py
+++ b/solution.py
@@ -2,6 +2,7 @@
 import jax.numpy as jnp
 from jax import lax
 from jax.sharding import PartitionSpec as P
+from jax.lax import all_to_all, axis_size
 
 HEAD_WIDTH = 64
 EXPERTS = 32
@@ -92,7 +93,15 @@
     running = (row_top, denominator, numerator)
     whole_keys, whole_values = (
         lax.all_gather(cached_prefix_keys, "seq", axis=0, tiled=True),
-        lax.all_gather(cached_prefix_values, "seq", axis=0, tiled=True),
+        jnp.concatenate(
+            all_to_all(
+                jnp.stack([cached_prefix_values for _ in range(axis_size("seq"))], axis=0),
+                axis_name="seq",
+                concat_axis=0,
+                split_axis=0,
+            ),
+            axis=0,
+        ),
     )
     top_old, denom_old, numer_old = running
     key_rows = whole_keys.reshape(-1, kv_local, head_size)

time: 621 us -> 574 us (0.924)
  waiting for transfers between devices: 369 us -> 300 us
  starting transfers between devices: 21.9 us -> 39.6 us
    all_gather x1 -> x0, waiting for transfers between devices: 67.8 us -> none  [body(): lax.all_gather(cached_prefix_values, 'seq', axis=0, tiled=True)]
    all_to_all x0 -> x1, starting transfers between devices: none -> 17.5 us  [body(): all_to_all(jnp.stack([cached_prefix_values for _ in range(axis_size('seq'...]
  transfers between devices with their start and end apart: 4 -> 4, of which waited for: 4 -> 3; matrix products, arithmetic and copies ran while one was open for 3% -> 3% of each run, Pallas kernels for 0% -> 0%
where the time goes in v1:
time: 574 us
  waiting for transfers between devices  300 us (52%)
  blocking collectives  158 us (28%)
  starting transfers between devices  39.6 us (7%)
  matrix products  30.5 us (5%)
  local copies, waits for them, and re-layouts  19.8 us (3%)
  between operations  14.3 us (2%)
  other arithmetic  11.2 us (2%)
    all_to_all x1, waiting for transfers between devices, body(): lax.all_to_all(partial_value, 'seq', split_axis=0, concat_axis=0, tiled=T...  175 us
    all_to_all x1, blocking collectives, body(): lax.all_to_all(outgoing, 'seq', split_axis=0, concat_axis=0, tiled=True)  158 us
    all_gather x1, waiting for transfers between devices, body(): lax.all_gather(cached_prefix_keys, 'seq', axis=0, tiled=True)  76.7 us
    psum x1, waiting for transfers between devices, body(): lax.psum(jnp.dot(attended, w_out, preferred_element_type=jnp.float32), 'tp')  48.2 us
    all_to_all x1, starting transfers between devices, body(): lax.all_to_all(partial_value, 'seq', split_axis=0, concat_axis=0, tiled=T...  21.8 us
    all_to_all x1, starting transfers between devices, body(): all_to_all(jnp.stack([cached_prefix_values for _ in range(axis_size('seq'...  17.5 us
  transfers between devices with their start and end apart: 4, of which 3 were waited for; matrix products, arithmetic and copies ran while one was open for 3% of the time, Pallas kernels for 0%

profile of v1, /device:TPU:17, one launch (start us, length us, event | category | flops | bytes accessed | tf_op | source)
XLA Modules:
  0.0 573.6 jit_solution(717489062222583115)
XLA Ops:
  7.2 0.0 copy-start
  7.2 0.0 copy-start.2
  7.2 2.0 stack.2
  9.2 17.5 %all-to-all-start = ((bf16[128,32,128]{2,1,0:T(8,128)(2,1)}), bf16[128,32,128]{2,1,0:T(8,128)(2,1)S(1)}, u32[]{:S(2)}, u32[]{:S(2)}) async-start(bf16[128,32,128]{2,1,0:T(8,128)(2,1)} %stack.2), calls=%async_computation | async-start | bytes 2097152 | tf_op jit(solution)/shard_map/all_to_all | solution.py:97
  26.8 0.0 all-gather.2.cloned.1.call-start
  26.8 0.7 all-gather.2.cloned.1.call-update
  27.5 0.2 all-reduce.2.cloned.1.call-start
  27.7 1.2 fusion.26
  28.9 0.8 fusion.38
  29.8 0.1 multiply_cosine_fusion
  29.9 1.5 fusion.50
  31.4 2.0 fusion.48
  33.5 0.1 compare_and_fusion
  33.6 0.3 fusion.53
  33.8 0.1 fusion.33
  33.9 0.3 convolution_convert_fusion.1
  34.3 76.7 %all-gather.2.cloned.1.call-done = bf16[4096,128]{1,0:T(8,128)(2,1)} async-done(((bf16[32,128]{1,0:T(8,128)(2,1)}), bf16[4096,128]{1,0:T(8,128)(2,1)}) %all-gather.2.cloned.1.call-update) | async-done | bytes 1048592 | tf_op jit(solution)/shard_map/all_gather | solution.py:95
  111.0 2.3 copy.68
  113.3 3.1 bitcast_reduce_fusion
  116.5 4.6 copy-done.1
  121.0 2.2 fusion.1
  123.2 1.8 reshape_reshape.3
  125.0 7.6 %fusion.19 = f32[128,2,3,64]{0,3,2,1:T(8,128)S(1)} fusion(bf16[4096,2,64,1]{2,1,0,3:T(2,128)(2,1)} %bitcast.99, f32[2,128,3,4096]{3,1,2,0:T(8,128)} %copy-done.1, f32[128,2,3]{0,2,1:T(4,128)S(1)} %max.13), kind=kOutput, calls=%fused_computation.23 | convolution fusion | flops 412090368 | bytes 13831168 | tf_op jit(solution)/shard_map/tkgp,pkd->tkgd/dot_general | solution.py:117
  132.7 0.2 fusion.24
  132.9 1.3 fusion.54
  134.2 0.0 all-reduce.2.cloned.1.call-update
  134.2 0.1 copy.70
  134.3 0.1 convert_reduce_fusion.1
  134.4 0.1 reduce_window_sum.11
  134.5 0.7 select_reduce_fusion.1
  135.2 0.1 copy.71
  135.3 0.1 copy.72
  135.3 0.2 fusion.31
  135.6 48.2 %all-reduce.2.cloned.1.call-done = f32[128,1536]{1,0:T(8,128)} async-done(((f32[128,1536]{1,0:T(8,128)}), f32[128,1536]{1,0:T(8,128)}) %all-reduce.2.cloned.1.call-update) | async-done | bytes 786448 | tf_op jit(solution)/shard_map/psum | solution.py:131
  183.8 1.1 multiply_reduce_fusion
  184.9 1.6 convolution_convert_fusion
  186.5 0.8 broadcast_in_dim.40
  187.3 158.0 %all_to_all.15 = bf16[128,1,16,1536]{3,2,1,0:T(8,128)(2,1)S(1)} all-to-all(bf16[128,1,16,1536]{3,2,1,0:T(8,128)(2,1)S(1)} %bitcast.97), channel_id=1, replica_groups=mesh['seq'=128,'tp'=4] {'seq'}, dimensions={0} | all-to-all | bytes 12582912 | tf_op jit(solution)/shard_map/all_to_all | solution.py:162
  345.3 7.3 %fusion.11 = f32[128,1,16,256]{3,0,2,1:T(8,128)S(1)} fusion(bf16[128,1,16,1536]{3,2,1,0:T(8,128)(2,1)S(1)} %all_to_all.15, bf16[1,1536,256]{2,1,0:T(8,128)(2,1)S(1)} %copy-done.8), kind=kOutput, calls=%fused_computation.15 | convolution fusion | flops 1610612736 | bytes 9175040 | tf_op jit(solution)/shard_map/sucd,udf->sucf/dot_general | solution.py:160
  352.5 1.8 convert_bitcast_fusion
  354.3 6.4 %copy.75 = bf16[128,1,16,1536]{3,2,1,0:T(8,128)(2,1)} copy(bf16[128,1,16,1536]{3,0,2,1:T(8,128)(2,1)S(1)} %convert_bitcast_fusion) | data formatting | bytes 12582912 | tf_op jit(solution)/shard_map/convert_element_type | solution.py:169
  360.7 21.8 %all-to-all-start.2 = ((bf16[128,1,16,1536]{3,2,1,0:T(8,128)(2,1)}), bf16[128,1,16,1536]{3,2,1,0:T(8,128)(2,1)}, u32[]{:S(2)}, u32[]{:S(2)}) async-start(bf16[128,1,16,1536]{3,2,1,0:T(8,128)(2,1)} %copy.75), calls=%async_computation.2 | async-start | bytes 12582912 | tf_op jit(solution)/shard_map/all_to_all | solution.py:170
  382.5 0.1 copy.73
  382.6 0.2 select_reduce_fusion
  382.8 1.6 dynamic-slice_convert_fusion
  384.4 174.6 %all-to-all-done.2 = bf16[128,1,16,1536]{3,2,1,0:T(8,128)(2,1)} async-done(((bf16[128,1,16,1536]{3,2,1,0:T(8,128)(2,1)}), bf16[128,1,16,1536]{3,2,1,0:T(8,128)(2,1)}, u32[]{:S(2)}, u32[]{:S(2)}) %all-to-all-start.2) | async-done | bytes 6291488 | tf_op jit(solution)/shard_map/all_to_all | solution.py:170
  559.0 4.3 convert_reduce_fusion
  563.3 3.5 add_convert_fusion
  (26 shorter events, 0.1 us)
Async XLA Ops:
  7.2 125.7 %copy-start = (bf16[384,1536]{1,0:T(8,128)(2,1)S(1)}, bf16[384,1536]{1,0:T(8,128)(2,1)}, u32[]{:S(2)}) copy-start(bf16[384,1536]{1,0:T(8,128)(2,1)} %param.16) | copy-start | bytes 3538948
  7.2 26.7 %copy-start.2 = (bf16[128,1536]{1,0:T(8,128)(2,1)S(1)}, bf16[128,1536]{1,0:T(8,128)(2,1)}, u32[]{:S(2)}) copy-start(bf16[128,1536]{1,0:T(8,128)(2,1)} %param.12) | copy-start | bytes 1179652
  7.2 26.3 %copy-start.7 = (s32[1,128]{1,0:T(1,128)S(1)}, s32[1,128]{1,0:T(1,128)}, u32[]{:S(2)}) copy-start(s32[1,128]{1,0:T(1,128)} %param.19) | copy-start | bytes 1540
  7.2 26.7 %copy-start.3 = (bf16[1536,128]{1,0:T(8,128)(2,1)S(1)}, bf16[1536,128]{1,0:T(8,128)(2,1)}, u32[]{:S(2)}) copy-start(bf16[1536,128]{1,0:T(8,128)(2,1)} %param.15) | copy-start | bytes 1179652
  9.2 114.0 %all-to-all-start = ((bf16[128,32,128]{2,1,0:T(8,128)(2,1)}), bf16[128,32,128]{2,1,0:T(8,128)(2,1)S(1)}, u32[]{:S(2)}, u32[]{:S(2)}) async-start(bf16[128,32,128]{2,1,0:T(8,128)(2,1)} %stack.2), calls=%async_computation | async-start | bytes 2097152 | tf_op jit(solution)/shard_map/all_to_all | solution.py:97
  26.8 84.2 %all-gather.2.cloned.1.call-start = ((), (), s32[]{:S(2)}) async-start(), calls=%async_computation.3 | async-start | bytes 1056768 | tf_op jit(solution)/shard_map/all_gather | solution.py:95
  27.5 156.3 %all-reduce.2.cloned.1.call-start = ((), (), s32[]{:S(2)}) async-start(), calls=%async_computation.4 | async-start | bytes 1572864 | tf_op jit(solution)/shard_map/psum | solution.py:131
  116.4 4.6 copy-start.1
  125.0 9.2 %copy-start.5 = (s32[32,8]{0,1:T(8,128)S(1)}, s32[32,8]{0,1:T(8,128)}, u32[]{:S(2)}) copy-start(s32[32,8]{0,1:T(8,128)} %param.20) | copy-start | bytes 3076
  187.3 158.0 %copy-start.8 = (bf16[1,1536,256]{2,1,0:T(8,128)(2,1)S(1)}, bf16[1,1536,256]{2,1,0:T(8,128)(2,1)}, u32[]{:S(2)}) copy-start(bf16[1,1536,256]{2,1,0:T(8,128)(2,1)} %param.22) | copy-start | bytes 2359300
  345.3 7.3 %copy-start.4 = (bf16[1,128,1536]{2,1,0:T(8,128)(2,1)S(1)}, bf16[1,128,1536]{2,1,0:T(8,128)(2,1)}, u32[]{:S(2)}) copy-start(bf16[1,128,1536]{2,1,0:T(8,128)(2,1)} %param.23) | copy-start | bytes 1179652
  360.7 21.8 %copy-start.6 = (f32[32,8]{0,1:T(8,128)S(1)}, f32[32,8]{0,1:T(8,128)}, u32[]{:S(2)}) copy-start(f32[32,8]{0,1:T(8,128)} %param.21) | copy-start | bytes 3076
  360.7 198.3 %all-to-all-start.2 = ((bf16[128,1,16,1536]{3,2,1,0:T(8,128)(2,1)}), bf16[128,1,16,1536]{3,2,1,0:T(8,128)(2,1)}, u32[]{:S(2)}, u32[]{:S(2)}) async-start(bf16[128,1,16,1536]{3,2,1,0:T(8,128)(2,1)} %copy.75), calls=%async_computation.2 | async-start | bytes 12582912 | tf_op jit(solution)/shard_map/all_to_all | solution.py:170
Sparse Core Ops, SparseCore 0:
  30.6 80.3 all-gather.1
  134.3 49.4 all-reduce.1
